TPU v7x, 32 devices: a whole 2x2x4 slice. The times are simulated.
32 devices in a mesh: dp: 4 (over y, x), expert: 8 (over z, core).
Axes of the slice: x: 2, y: 2, z: 4, core: 2. Of those that a mesh axis runs over, the one named last changes fastest.
Arguments:
- tokens: bfloat16 [4096, 3584], P(('dp', 'expert')), may hold values from -6 to 6
- gate_probs: float32 [4096, 8], P(('dp', 'expert')), may hold values from 0.1 to 1
- expert_ids: int32 [4096, 8], P(('dp', 'expert')), may hold values from 0 to 63, all different within a row; in each aligned block of 128 rows (0 to 127, 128 to 255, ...) at most 24 rows name the same one
- cotangent: bfloat16 [4096, 3584], P(('dp', 'expert')), may hold values from -6 to 6
- w_gate: bfloat16 [8, 3584, 2048], P('expert', None, 'dp'), may hold values from -0.09375 to 0.09375
- w_up: bfloat16 [8, 3584, 2048], P('expert', None, 'dp'), may hold values from -0.09375 to 0.09375
- w_down: bfloat16 [8, 2048, 3584], P('expert', 'dp'), may hold values from -0.125 to 0.125
Outputs:
- layer_out: bfloat16 [4096, 3584], P(('dp', 'expert'))
- grad_tokens: bfloat16 [4096, 3584], P(('dp', 'expert'))
- grad_probs: float32 [4096, 8], P(('dp', 'expert'))
- grad_gate: bfloat16 [8, 3584, 2048], P('expert', None, 'dp')
- grad_up: bfloat16 [8, 3584, 2048], P('expert', None, 'dp')
- grad_down: bfloat16 [8, 2048, 3584], P('expert', 'dp')
Inputs may be any that keep to these rules, and one draw needn't show every extreme that they name: `expert_ids`: each token names 8 distinct ids. Among the 128 tokens of one device no id is named by more than 24 of them, a bound that some block reaches. Only ids below 8 belong to the window.
All inputs are finite; a program needn't handle non-finite values.
Results may differ from a plain program's by a relative error of at most 0.012.
Values may be sent and summed in bfloat16 or wider, within the bound.
No kernel may reach another device: no remote copies, remote signals or barrier semaphores. Data moves between devices by JAX's collectives and lax.ppermute only.
A program may use at most 192 MiB of HBM per device.

v0:
```python
import jax
import jax.numpy as jnp
from jax import lax
from jax.sharding import PartitionSpec as P


def slot_table(flat_ids, experts, capacity, sentinel):
    matches = (flat_ids[:, None] == jnp.arange(experts, dtype=jnp.int32)[None, :]).astype(jnp.int32)
    earlier = jnp.cumsum(matches, axis=0) - matches
    slot_pos = jnp.sum(earlier * matches, axis=1)
    target = jnp.where(flat_ids < experts, flat_ids * capacity + slot_pos, experts * capacity)
    flat_index = jnp.arange(flat_ids.shape[0], dtype=jnp.int32)
    blank_table = jnp.full((experts * capacity,), sentinel, jnp.int32)
    return blank_table.at[target].set(flat_index, mode="drop")


def contract_last(left, right):
    return lax.dot_general(
        left, right, (((1,), (1,)), ((), ())), preferred_element_type=jnp.float32
    )


def contract_first(left, right):
    return lax.dot_general(
        left, right, (((0,), (0,)), ((), ())), preferred_element_type=jnp.float32
    )


def dispatch(send_rows):
    along_expert = lax.all_to_all(send_rows, "expert", split_axis=0, concat_axis=0, tiled=True)
    return lax.all_gather(along_expert, "dp", axis=0, tiled=True)


def gather_back(partial_rows, groups):
    summed = lax.psum_scatter(partial_rows, "dp", scatter_dimension=0, tiled=True)
    return lax.all_to_all(summed, "expert", split_axis=0, concat_axis=0, tiled=True)


def expert_forward(rows_x, gate_w, up_w, down_w):
    gate_pre = jnp.dot(rows_x, gate_w, preferred_element_type=jnp.float32)
    up_pre = jnp.dot(rows_x, up_w, preferred_element_type=jnp.float32)
    hidden = (gate_pre * jax.nn.sigmoid(gate_pre) * up_pre).astype(jnp.bfloat16)
    part_out = jnp.dot(hidden, down_w, preferred_element_type=jnp.float32).astype(jnp.bfloat16)
    return lax.optimization_barrier((part_out, hidden, gate_pre, up_pre))


def expert_backward(rows_c, gate_pre, up_pre, gate_w, up_w, down_w):
    sigmoid_g = jax.nn.sigmoid(gate_pre)
    activated = gate_pre * sigmoid_g
    grad_hidden = contract_last(rows_c, down_w)
    grad_upin = (grad_hidden * activated).astype(jnp.bfloat16)
    grad_gatein = (grad_hidden * up_pre * sigmoid_g * (1.0 + gate_pre * (1.0 - sigmoid_g))).astype(
        jnp.bfloat16
    )
    part_dx = (contract_last(grad_gatein, gate_w) + contract_last(grad_upin, up_w)).astype(
        jnp.bfloat16
    )
    return (part_dx, grad_gatein, grad_upin)


def join_slots(chunks, experts, model_width):
    parts = [chunk.reshape(experts, -1, model_width) for chunk in chunks]
    return jnp.concatenate(parts, axis=1).reshape(-1, model_width)


def on_device(tokens, gate_probs, expert_ids, cotangent, w_gate, w_up, w_down):
    tok_count, model_width = tokens.shape
    top_k = expert_ids.shape[1]
    experts = lax.axis_size("expert")
    groups = lax.axis_size("dp")
    capacity = 3 * tok_count * top_k // (16 * experts)
    flat_count = tok_count * top_k
    slots = slot_table(expert_ids.reshape(-1), experts, capacity, flat_count)
    token_of = slots // top_k
    zero_row = jnp.zeros((1, model_width), jnp.bfloat16)
    send_x = jnp.concatenate([tokens, zero_row], 0)[token_of]
    rows_dy = jnp.concatenate([cotangent, zero_row], 0)[token_of]
    prob_rows = jnp.concatenate([gate_probs.reshape(-1), jnp.zeros((1,), jnp.float32)], 0)[slots]
    send_c = (prob_rows[:, None] * rows_dy.astype(jnp.float32)).astype(jnp.bfloat16)
    half = max(capacity // 2, 1)
    bounds = [(lo, hi) for lo, hi in ((0, half), (half, capacity)) if hi > lo]
    x_by_slot = send_x.reshape(experts, capacity, model_width)
    c_by_slot = send_c.reshape(experts, capacity, model_width)
    xs = [dispatch(x_by_slot[:, lo:hi].reshape(-1, model_width)) for lo, hi in bounds]
    cs = [dispatch(c_by_slot[:, lo:hi].reshape(-1, model_width)) for lo, hi in bounds]
    gate_w = w_gate[0]
    up_w = w_up[0]
    down_w = w_down[0]
    forwards = [expert_forward(rows_x, gate_w, up_w, down_w) for rows_x in xs]
    outs = [gather_back(fw[0], groups) for fw in forwards]
    backwards = [
        expert_backward(rows_c, fw[2], fw[3], gate_w, up_w, down_w)
        for rows_c, fw in zip(cs, forwards)
    ]
    dxs = [gather_back(bw[0], groups) for bw in backwards]
    new_gate = sum((contract_first(rx, bw[1]) for rx, bw in zip(xs, backwards)))
    new_up = sum((contract_first(rx, bw[2]) for rx, bw in zip(xs, backwards)))
    new_down = sum((contract_first(fw[1], rc) for fw, rc in zip(forwards, cs)))
    new_gate = new_gate.astype(jnp.bfloat16)[None]
    new_up = new_up.astype(jnp.bfloat16)[None]
    new_down = new_down.astype(jnp.bfloat16)[None]
    out_rows = join_slots(outs, experts, model_width).astype(jnp.float32)
    dx_rows = join_slots(dxs, experts, model_width).astype(jnp.float32)
    owner = (token_of[None, :] == jnp.arange(tok_count, dtype=jnp.int32)[:, None]).astype(
        jnp.float32
    )
    layer_out = jnp.dot(
        owner * prob_rows[None, :],
        out_rows,
        precision=lax.Precision.HIGHEST,
        preferred_element_type=jnp.float32,
    ).astype(jnp.bfloat16)
    grad_tokens = jnp.dot(
        owner, dx_rows, precision=lax.Precision.HIGHEST, preferred_element_type=jnp.float32
    ).astype(jnp.bfloat16)
    score_rows = jnp.sum(rows_dy.astype(jnp.float32) * out_rows, axis=1)
    grad_probs = (
        jnp.zeros((flat_count + 1,), jnp.float32)
        .at[slots]
        .set(score_rows)[:flat_count]
        .reshape(tok_count, top_k)
    )
    return (layer_out, grad_tokens, grad_probs, new_gate, new_up, new_down)


def solution(mesh):
    return jax.shard_map(
        on_device,
        mesh=mesh,
        in_specs=(
            P(("dp", "expert"), None),
            P(("dp", "expert"), None),
            P(("dp", "expert"), None),
            P(("dp", "expert"), None),
            P("expert", None, "dp"),
            P("expert", None, "dp"),
            P("expert", "dp", None),
        ),
        out_specs=(
            P(("dp", "expert"), None),
            P(("dp", "expert"), None),
            P(("dp", "expert"), None),
            P("expert", None, "dp"),
            P("expert", None, "dp"),
            P("expert", "dp", None),
        ),
        check_vma=False,
    )
```

profile of v0, /device:TPU:0, one launch (start us, length us, event | category | flops | bytes accessed | tf_op | source)
XLA Modules:
  0.0 435.6 jit_solution(945280252774466416)
XLA Ops:
  10.0 2.3 reduce-window.6
  12.9 4.3 scatter_custom_fusion
  17.2 1.2 concatenate.16
  18.5 1.4 gather_fusion.1
  20.1 29.9 %all_to_all.72 = bf16[8,12,3584]{2,1,0:T(8,128)(2,1)S(1)} all-to-all(bf16[8,12,3584]{2,1,0:T(8,128)(2,1)S(1)} %get-tuple-element.37), channel_id=1, replica_groups=mesh['dp'=4,'expert'=8] {'expert'}, dimensions={0} | all-to-all | bytes 1376256 | tf_op jit(solution)/shard_map/all_to_all | solution.py:30
  51.1 26.3 %all_to_all.73 = bf16[8,12,3584]{2,1,0:T(8,128)(2,1)S(1)} all-to-all(bf16[8,12,3584]{2,1,0:T(8,128)(2,1)S(1)} %get-tuple-element.36), channel_id=1, replica_groups=mesh['dp'=4,'expert'=8] {'expert'}, dimensions={0} | all-to-all | bytes 1376256 | tf_op jit(solution)/shard_map/all_to_all | solution.py:30
  78.8 1.4 gather_fusion
  80.4 1.4 gather_fusion.2
  82.9 26.2 %all_to_all.74 = bf16[8,12,3584]{2,1,0:T(8,128)(2,1)S(1)} all-to-all(bf16[8,12,3584]{2,1,0:T(8,128)(2,1)S(1)} %get-tuple-element.34), channel_id=1, replica_groups=mesh['dp'=4,'expert'=8] {'expert'}, dimensions={0} | all-to-all | bytes 1376256 | tf_op jit(solution)/shard_map/all_to_all | solution.py:30
  110.1 26.2 %all_to_all.75 = bf16[8,12,3584]{2,1,0:T(8,128)(2,1)S(1)} all-to-all(bf16[8,12,3584]{2,1,0:T(8,128)(2,1)S(1)} %get-tuple-element.35), channel_id=1, replica_groups=mesh['dp'=4,'expert'=8] {'expert'}, dimensions={0} | all-to-all | bytes 1376256 | tf_op jit(solution)/shard_map/all_to_all | solution.py:30
  137.4 4.6 %fusion.21 = f32[384,512]{1,0:T(8,128)S(1)} fusion(bf16[384,3584]{1,0:T(8,128)(2,1)} %all-gather.7.cloned.1.call-done, bf16[1,3584,512]{2,1,0:T(8,128)(2,1)} %param.11), kind=kOutput, calls=%fused_computation.35 | convolution fusion | flops 1409286144 | bytes 7208960 | tf_op jit(solution)/shard_map/dot_general | solution.py:40
  142.2 2.5 multiply_convert_fusion.5
  145.4 3.1 convolution_convert_fusion
  148.9 4.6 %fusion.23 = f32[384,512]{1,0:T(8,128)S(1)} fusion(bf16[384,3584]{1,0:T(8,128)(2,1)} %all-gather.5.cloned.1.call-done, bf16[1,3584,512]{2,1,0:T(8,128)(2,1)} %param.11), kind=kOutput, calls=%fused_computation.37 | convolution fusion | flops 1409286144 | bytes 7208960 | tf_op jit(solution)/shard_map/dot_general | solution.py:40
  153.6 2.5 multiply_convert_fusion.6
  156.8 3.1 convolution_convert_fusion.1
  160.1 16.6 %all-gather.9.cloned.1.call-done = bf16[384,3584]{1,0:T(8,128)(2,1)} async-done(((bf16[96,3584]{1,0:T(8,128)(2,1)}), bf16[384,3584]{1,0:T(8,128)(2,1)}) %all-gather.9.cloned.1.call-update) | async-done | bytes 2752528 | tf_op jit(solution)/shard_map/all_gather | solution.py:31
  176.7 5.2 %multiply_convert_fusion.3 = (bf16[384,512]{1,0:T(8,128)(2,1)S(1)}, bf16[384,512]{1,0:T(8,128)(2,1)S(1)}) fusion(f32[384,512]{1,0:T(8,128)} %copy-done.24, f32[384,512]{1,0:T(8,128)} %get-tuple-element.16, bf16[384,3584]{1,0:T(8,128)(2,1)} %all-gather.9.cloned.1.call-done, bf16[1,512,3584]{2,1,0:T(8,128)(2,1)} %param.13), kind=kOutput, calls=%fused_computation.46 | convolution fusion | flops 1411842048 | bytes 8781824 | tf_op jit(solution)/shard_map/dot_general | solution.py:18
  181.9 1.6 fusion.19
  183.9 3.2 fusion
  187.2 32.0 %all-gather.11.cloned.1.call-done = bf16[384,3584]{1,0:T(8,128)(2,1)} async-done(((bf16[96,3584]{1,0:T(8,128)(2,1)}), bf16[384,3584]{1,0:T(8,128)(2,1)}) %all-gather.11.cloned.1.call-update) | async-done | bytes 2752528 | tf_op jit(solution)/shard_map/all_gather | solution.py:31
  219.1 5.2 %multiply_convert_fusion.1 = (bf16[384,512]{1,0:T(8,128)(2,1)S(1)}, bf16[384,512]{1,0:T(8,128)(2,1)S(1)}) fusion(f32[384,512]{1,0:T(8,128)} %copy-done.23, f32[384,512]{1,0:T(8,128)} %get-tuple-element.18, bf16[384,3584]{1,0:T(8,128)(2,1)} %all-gather.11.cloned.1.call-done, bf16[1,512,3584]{2,1,0:T(8,128)(2,1)} %param.13), kind=kOutput, calls=%fused_computation.43 | convolution fusion | flops 1411842048 | bytes 8781824 | tf_op jit(solution)/shard_map/dot_general | solution.py:18
  224.4 1.6 fusion.17
  226.7 3.2 fusion.1
  229.9 33.3 %reduce-scatter.7.cloned.1.call-done = bf16[96,3584]{1,0:T(8,128)(2,1)} async-done(((bf16[384,3584]{1,0:T(8,128)(2,1)}), bf16[96,3584]{1,0:T(8,128)(2,1)}) %reduce-scatter.7.cloned.1.call-update) | async-done | bytes 688144 | tf_op jit(solution)/shard_map/reduce_scatter | solution.py:35
  263.3 2.1 all_to_all.54
  265.4 4.6 %all-to-all-start.3 = ((bf16[8,12,3584]{2,1,0:T(8,128)(2,1)}), bf16[8,12,3584]{2,1,0:T(8,128)(2,1)}, u32[]{:S(2)}, u32[]{:S(2)}) async-start(bf16[8,12,3584]{2,1,0:T(8,128)(2,1)} %all_to_all.54), calls=%async_computation.5 | async-start | bytes 1835008 | tf_op jit(solution)/shard_map/all_to_all | solution.py:36
  270.0 37.5 %reduce-scatter.5.cloned.1.call-done = bf16[96,3584]{1,0:T(8,128)(2,1)} async-done(((bf16[384,3584]{1,0:T(8,128)(2,1)}), bf16[96,3584]{1,0:T(8,128)(2,1)}) %reduce-scatter.5.cloned.1.call-update) | async-done | bytes 688144 | tf_op jit(solution)/shard_map/reduce_scatter | solution.py:35
  307.4 2.1 all_to_all.50
  309.5 4.6 %all-to-all-start.1 = ((bf16[8,12,3584]{2,1,0:T(8,128)(2,1)}), bf16[8,12,3584]{2,1,0:T(8,128)(2,1)}, u32[]{:S(2)}, u32[]{:S(2)}) async-start(bf16[8,12,3584]{2,1,0:T(8,128)(2,1)} %all_to_all.50), calls=%async_computation.2 | async-start | bytes 1835008 | tf_op jit(solution)/shard_map/all_to_all | solution.py:36
  314.1 3.9 fusion.42
  318.1 4.1 fusion.3
  322.1 29.6 %reduce-scatter.9.cloned.1.call-done = bf16[96,3584]{1,0:T(8,128)(2,1)} async-done(((bf16[384,3584]{1,0:T(8,128)(2,1)}), bf16[96,3584]{1,0:T(8,128)(2,1)}) %reduce-scatter.9.cloned.1.call-update) | async-done | bytes 688144 | tf_op jit(solution)/shard_map/reduce_scatter | solution.py:35
  351.7 2.1 all_to_all.58
  353.8 4.6 %all-to-all-start.5 = ((bf16[8,12,3584]{2,1,0:T(8,128)(2,1)}), bf16[8,12,3584]{2,1,0:T(8,128)(2,1)}, u32[]{:S(2)}, u32[]{:S(2)}) async-start(bf16[8,12,3584]{2,1,0:T(8,128)(2,1)} %all_to_all.58), calls=%async_computation.8 | async-start | bytes 1835008 | tf_op jit(solution)/shard_map/all_to_all | solution.py:36
  358.4 4.0 fusion.41
  362.5 5.0 %fusion.43 = f32[512,3584]{1,0:T(8,128)} fusion(bf16[384,512]{1,0:T(8,128)(2,1)S(1)} %copy-done.19, bf16[384,3584]{1,0:T(8,128)(2,1)S(1)} %copy-done.10), kind=kOutput, calls=%fused_computation.87 | convolution fusion | flops 1409286144 | bytes 10485760 | tf_op jit(solution)/shard_map/dot_general | solution.py:24
  367.5 4.1 fusion.2
  371.5 23.9 %reduce-scatter.11.cloned.1.call-done = bf16[96,3584]{1,0:T(8,128)(2,1)} async-done(((bf16[384,3584]{1,0:T(8,128)(2,1)}), bf16[96,3584]{1,0:T(8,128)(2,1)}) %reduce-scatter.11.cloned.1.call-update) | async-done | bytes 688144 | tf_op jit(solution)/shard_map/reduce_scatter | solution.py:35
  395.4 2.1 all_to_all.62
  397.5 4.6 %all-to-all-start.7 = ((bf16[8,12,3584]{2,1,0:T(8,128)(2,1)}), bf16[8,12,3584]{2,1,0:T(8,128)(2,1)S(1)}, u32[]{:S(2)}, u32[]{:S(2)}) async-start(bf16[8,12,3584]{2,1,0:T(8,128)(2,1)} %all_to_all.62), calls=%async_computation.11 | async-start | bytes 1835008 | tf_op jit(solution)/shard_map/all_to_all | solution.py:36
  402.1 7.9 %fusion.4 = bf16[1,512,3584]{2,1,0:T(8,128)(2,1)} fusion(f32[512,3584]{1,0:T(8,128)} %fusion.43, bf16[384,512]{1,0:T(8,128)(2,1)S(1)} %copy-done.17, bf16[384,3584]{1,0:T(8,128)(2,1)} %all-gather.11.cloned.1.call-done), kind=kOutput, calls=%fused_computation.16 | convolution fusion | flops 1412956160 | bytes 14155776 | tf_op jit(solution)/shard_map/dot_general | solution.py:24
  410.0 1.9 pad_maximum_fusion
  412.3 1.2 scatter_custom_fusion.1
  414.3 1.8 convolution_convert_fusion.3
  416.1 9.8 %all-to-all-done.7 = bf16[8,12,3584]{2,1,0:T(8,128)(2,1)S(1)} async-done(((bf16[8,12,3584]{2,1,0:T(8,128)(2,1)}), bf16[8,12,3584]{2,1,0:T(8,128)(2,1)S(1)}, u32[]{:S(2)}, u32[]{:S(2)}) %all-to-all-start.7) | async-done | bytes 688160 | tf_op jit(solution)/shard_map/all_to_all | solution.py:36
  425.9 1.5 pad_maximum_fusion.1
  427.4 1.3 convolution_convert_fusion.2
  (106 shorter events, 13.9 us)
Async XLA Ops:
  7.2 130.3 %all-gather.7.cloned.1.call-start = ((), (), s32[]{:S(2)}) async-start(), calls=%async_computation.14 | async-start | bytes 3440640 | tf_op jit(solution)/shard_map/all_gather | solution.py:31
  51.0 27.5 %copy-start.20 = (f32[128,8]{0,1:T(8,128)S(1)}, f32[128,8]{0,1:T(8,128)}, u32[]{:S(2)}) copy-start(f32[128,8]{0,1:T(8,128)} %param.8) | copy-start | bytes 12292
  51.1 29.2 %copy-start.15 = (bf16[128,3584]{1,0:T(8,128)(2,1)S(1)}, bf16[128,3584]{1,0:T(8,128)(2,1)}, u32[]{:S(2)}) copy-start(bf16[128,3584]{1,0:T(8,128)(2,1)} %param.10) | copy-start | bytes 2752516
  51.1 97.8 %all-gather.5.cloned.1.call-start = ((), (), s32[]{:S(2)}) async-start(), calls=%async_computation.12 | async-start | bytes 3440640 | tf_op jit(solution)/shard_map/all_gather | solution.py:31
  78.5 98.2 %all-gather.9.cloned.1.call-start = ((), (), s32[]{:S(2)}) async-start(), calls=%async_computation.16 | async-start | bytes 3440640 | tf_op jit(solution)/shard_map/all_gather | solution.py:31
  81.8 1.1 copy-start.8
  110.1 109.0 %all-gather.11.cloned.1.call-start = ((), (), s32[]{:S(2)}) async-start(), calls=%async_computation.18 | async-start | bytes 3440640 | tf_op jit(solution)/shard_map/all_gather | solution.py:31
  137.4 125.9 %reduce-scatter.7.cloned.1.call-start = ((), (), s32[]{:S(2)}) async-start(), calls=%async_computation.15 | async-start | bytes 3440640 | tf_op jit(solution)/shard_map/reduce_scatter | solution.py:35
  137.4 4.6 %copy-start = (bf16[384,3584]{1,0:T(8,128)(2,1)S(1)}, bf16[384,3584]{1,0:T(8,128)(2,1)}, u32[]{:S(2)}) copy-start(bf16[384,3584]{1,0:T(8,128)(2,1)} %all-gather.7.cloned.1.call-done) | copy-start | bytes 8257540
  137.4 4.8 %copy-start.3 = (bf16[1,3584,512]{2,1,0:T(8,128)(2,1)S(1)}, bf16[1,3584,512]{2,1,0:T(8,128)(2,1)}, u32[]{:S(2)}) copy-start(bf16[1,3584,512]{2,1,0:T(8,128)(2,1)} %param.12) | copy-start | bytes 11010052
  142.2 2.5 copy-start.23
  142.2 3.2 copy-start.21
  144.7 0.8 copy-start.16
  148.6 158.8 %reduce-scatter.5.cloned.1.call-start = ((), (), s32[]{:S(2)}) async-start(), calls=%async_computation.13 | async-start | bytes 3440640 | tf_op jit(solution)/shard_map/reduce_scatter | solution.py:35
  148.8 4.6 %copy-start.4 = (bf16[1,3584,512]{2,1,0:T(8,128)(2,1)S(1)}, bf16[1,3584,512]{2,1,0:T(8,128)(2,1)}, u32[]{:S(2)}) copy-start(bf16[1,3584,512]{2,1,0:T(8,128)(2,1)} %param.12) | copy-start | bytes 11010052
  148.9 4.8 %copy-start.7 = (bf16[384,3584]{1,0:T(8,128)(2,1)S(1)}, bf16[384,3584]{1,0:T(8,128)(2,1)}, u32[]{:S(2)}) copy-start(bf16[384,3584]{1,0:T(8,128)(2,1)} %all-gather.5.cloned.1.call-done) | copy-start | bytes 8257540
  153.6 2.5 copy-start.24
  153.6 3.2 copy-start.22
  156.1 0.7 copy-start.18
  160.0 191.7 %reduce-scatter.9.cloned.1.call-start = ((), (), s32[]{:S(2)}) async-start(), calls=%async_computation.17 | async-start | bytes 3440640 | tf_op jit(solution)/shard_map/reduce_scatter | solution.py:35
  176.7 5.2 %copy-start.1 = (bf16[1,3584,512]{2,1,0:T(8,128)(2,1)S(1)}, bf16[1,3584,512]{2,1,0:T(8,128)(2,1)}, u32[]{:S(2)}) copy-start(bf16[1,3584,512]{2,1,0:T(8,128)(2,1)} %param.11) | copy-start | bytes 11010052
  181.9 2.0 copy-start.5
  187.1 208.3 %reduce-scatter.11.cloned.1.call-start = ((), (), s32[]{:S(2)}) async-start(), calls=%async_computation.19 | async-start | bytes 3440640 | tf_op jit(solution)/shard_map/reduce_scatter | solution.py:35
  219.1 5.2 %copy-start.2 = (bf16[1,3584,512]{2,1,0:T(8,128)(2,1)S(1)}, bf16[1,3584,512]{2,1,0:T(8,128)(2,1)}, u32[]{:S(2)}) copy-start(bf16[1,3584,512]{2,1,0:T(8,128)(2,1)} %param.11) | copy-start | bytes 11010052
  224.3 1.7 copy-start.11
  224.3 1.7 copy-start.13
  224.4 2.3 copy-start.6
  265.4 44.1 %all-to-all-start.3 = ((bf16[8,12,3584]{2,1,0:T(8,128)(2,1)}), bf16[8,12,3584]{2,1,0:T(8,128)(2,1)}, u32[]{:S(2)}, u32[]{:S(2)}) async-start(bf16[8,12,3584]{2,1,0:T(8,128)(2,1)} %all_to_all.54), calls=%async_computation.5 | async-start | bytes 1835008 | tf_op jit(solution)/shard_map/all_to_all | solution.py:36
  309.5 44.3 %all-to-all-start.1 = ((bf16[8,12,3584]{2,1,0:T(8,128)(2,1)}), bf16[8,12,3584]{2,1,0:T(8,128)(2,1)}, u32[]{:S(2)}, u32[]{:S(2)}) async-start(bf16[8,12,3584]{2,1,0:T(8,128)(2,1)} %all_to_all.50), calls=%async_computation.2 | async-start | bytes 1835008 | tf_op jit(solution)/shard_map/all_to_all | solution.py:36
  314.1 3.9 copy-start.14
  353.8 43.7 %all-to-all-start.5 = ((bf16[8,12,3584]{2,1,0:T(8,128)(2,1)}), bf16[8,12,3584]{2,1,0:T(8,128)(2,1)}, u32[]{:S(2)}, u32[]{:S(2)}) async-start(bf16[8,12,3584]{2,1,0:T(8,128)(2,1)} %all_to_all.58), calls=%async_computation.8 | async-start | bytes 1835008 | tf_op jit(solution)/shard_map/all_to_all | solution.py:36
  358.4 4.0 copy-start.10
  358.4 4.1 copy-start.19
  362.4 5.0 %copy-start.12 = (bf16[384,512]{1,0:T(8,128)(2,1)S(1)}, bf16[384,512]{1,0:T(8,128)(2,1)}, u32[]{:S(2)}) copy-start(bf16[384,512]{1,0:T(8,128)(2,1)} %copy-done.11) | copy-start | bytes 1179652
  371.5 30.5 %copy-start.17 = (bf16[384,512]{1,0:T(8,128)(2,1)S(1)}, bf16[384,512]{1,0:T(8,128)(2,1)}, u32[]{:S(2)}) copy-start(bf16[384,512]{1,0:T(8,128)(2,1)} %copy-done.16) | copy-start | bytes 1179652
  397.5 28.4 %all-to-all-start.7 = ((bf16[8,12,3584]{2,1,0:T(8,128)(2,1)}), bf16[8,12,3584]{2,1,0:T(8,128)(2,1)S(1)}, u32[]{:S(2)}, u32[]{:S(2)}) async-start(bf16[8,12,3584]{2,1,0:T(8,128)(2,1)} %all_to_all.62), calls=%async_computation.11 | async-start | bytes 1835008 | tf_op jit(solution)/shard_map/all_to_all | solution.py:36
  410.0 1.9 copy-start.9
Sparse Core Ops, SparseCore 0:
  51.2 39.6 all-gather.6
  93.3 40.7 all-gather.4
  135.9 40.7 all-gather.8
  178.4 40.7 all-gather.10
  222.6 40.6 reduce-scatter.6
  266.7 40.6 reduce-scatter.4
  311.0 40.6 reduce-scatter.8
  354.7 40.6 reduce-scatter.10
where the time goes:
time: 436 us
  waiting for transfers between devices  183 us (42%)
  blocking collectives  109 us (25%)
  matrix products  72.5 us (17%)
  local copies, waits for them, and re-layouts  30.1 us (7%)
  starting transfers between devices  18.9 us (4%)
  between operations  14.6 us (3%)
  other arithmetic  8.13 us (2%)
    reduce_scatter x4, waiting for transfers between devices, gather_back(): lax.psum_scatter(partial_rows, 'dp', scatter_dimension=0, tiled=True)  124 us
    all_to_all x4, blocking collectives, dispatch(): lax.all_to_all(send_rows, 'expert', split_axis=0, concat_axis=0, tiled=True)  109 us
    all_gather x4, waiting for transfers between devices, dispatch(): return lax.all_gather(along_expert, 'dp', axis=0, tiled=True)  48.6 us
    dot_general x6, matrix products, contract_first(): lax.dot_general(left, right, (((0,), (0,)), ((), ())), preferred_element_...  29 us
    dot_general x6, matrix products, contract_last(): lax.dot_general(left, right, (((1,), (1,)), ((), ())), preferred_element_...  20 us
    all_to_all x4, starting transfers between devices, gather_back(): lax.all_to_all(summed, 'expert', split_axis=0, concat_axis=0, tiled=True)  18.4 us
    all_to_all x4, waiting for transfers between devices, gather_back(): lax.all_to_all(summed, 'expert', split_axis=0, concat_axis=0, tiled=True)  9.8 us
    dot_general x2, matrix products, expert_forward(): gate_pre = jnp.dot(rows_x, gate_w, preferred_element_type=jnp.float32)  9.19 us
  transfers between devices with their start and end apart: 12, of which 7 were waited for; matrix products, arithmetic and copies ran while one was open for 18% of the time, Pallas kernels for 0%

commit v1 on v0

--- a/solution.py
+++ b/solution.py
@@ -2,6 +2,19 @@
 import jax.numpy as jnp
 from jax import lax
 from jax.sharding import PartitionSpec as P
+
+
+def ring_gather(shard, axis, dim):
+    ways = lax.axis_size(axis)
+    up = [(d, (d + 1) % ways) for d in range(ways)]
+    down = [(d, (d - 1) % ways) for d in range(ways)]
+    earlier, later = ([shard], [shard])
+    for _ in range(ways // 2):
+        earlier.append(lax.ppermute(earlier[-1], axis, up))
+    for _ in range((ways - 1) // 2):
+        later.append(lax.ppermute(later[-1], axis, down))
+    line = jnp.concatenate([*earlier[::-1], *later[1:]], axis=dim)
+    return jnp.roll(line, (lax.axis_index(axis) - ways // 2) * shard.shape[dim], axis=dim)
 
 
 def slot_table(flat_ids, experts, capacity, sentinel):
@@ -28,7 +41,7 @@
 
 def dispatch(send_rows):
     along_expert = lax.all_to_all(send_rows, "expert", split_axis=0, concat_axis=0, tiled=True)
-    return lax.all_gather(along_expert, "dp", axis=0, tiled=True)
+    return ring_gather(along_expert, "dp", 0)
 
 
 def gather_back(partial_rows, groups):

time: 436 us -> 553 us (1.27)
  waiting for transfers between devices: 183 us -> 247 us
  other arithmetic: 8.13 us -> 54.4 us
  matrix products: 72.5 us -> 59 us
  starting transfers between devices: 18.9 us -> 30.3 us
    ppermute x0 -> x12, waiting for transfers between devices: none -> 193 us  [the longest x8 139 us: ring_gather(): earlier.append(lax.ppermute(earlier[-1], axis, up))]
    reduce_scatter x4, waiting for transfers between devices: 124 us -> 0.04 us  [gather_back(): lax.psum_scatter(partial_rows, 'dp', scatter_dimension=0, tiled=True)]
    all_gather x4 -> x0, waiting for transfers between devices: 48.6 us -> none  [dispatch(): return lax.all_gather(along_expert, 'dp', axis=0, tiled=True)]
    concatenate x0 -> x4, other arithmetic: none -> 45.1 us  [ring_gather(): jnp.roll(line, (lax.axis_index(axis) - ways // 2) * shard.shape[dim], axi...]
    all_to_all x4, waiting for transfers between devices: 9.8 us -> 54.2 us  [gather_back(): lax.all_to_all(summed, 'expert', split_axis=0, concat_axis=0, tiled=True)]
    ppermute x0 -> x12, starting transfers between devices: none -> 13.4 us  [the longest x4 9.66 us: ring_gather(): later.append(lax.ppermute(later[-1], axis, down))]
    dot_general x6, matrix products: 20 us -> 13.1 us  [contract_last(): lax.dot_general(left, right, (((1,), (1,)), ((), ())), preferred_element_...]
    dot_general x2, matrix products: 9.19 us -> 3.15 us  [expert_forward(): gate_pre = jnp.dot(rows_x, gate_w, preferred_element_type=jnp.float32)]
  transfers between devices with their start and end apart: 12 -> 20, of which waited for: 7 -> 16; matrix products, arithmetic and copies ran while one was open for 18% -> 17% of each run, Pallas kernels for 0% -> 0%
where the time goes in v1:
time: 553 us; the launch traced here: 548 us
  waiting for transfers between devices  247 us (45%)
  blocking collectives  110 us (20%)
  matrix products  59 us (11%)
  other arithmetic  54.4 us (10%)
  local copies, waits for them, and re-layouts  33.5 us (6%)
  starting transfers between devices  30.3 us (5%)
  between operations  14.8 us (3%)
    ppermute x8, waiting for transfers between devices, ring_gather(): earlier.append(lax.ppermute(earlier[-1], axis, up))  139 us
    all_to_all x4, blocking collectives, dispatch(): lax.all_to_all(send_rows, 'expert', split_axis=0, concat_axis=0, tiled=True)  110 us
    all_to_all x4, waiting for transfers between devices, gather_back(): lax.all_to_all(summed, 'expert', split_axis=0, concat_axis=0, tiled=True)  54.2 us
    ppermute x4, waiting for transfers between devices, ring_gather(): later.append(lax.ppermute(later[-1], axis, down))  53.8 us
    concatenate x4, other arithmetic, ring_gather(): jnp.roll(line, (lax.axis_index(axis) - ways // 2) * shard.shape[dim], axi...  45.1 us
    dot_general x6, matrix products, contract_first(): lax.dot_general(left, right, (((0,), (0,)), ((), ())), preferred_element_...  28.3 us
    all_to_all x4, starting transfers between devices, gather_back(): lax.all_to_all(summed, 'expert', split_axis=0, concat_axis=0, tiled=True)  16.7 us
    dot_general x6, matrix products, contract_last(): lax.dot_general(left, right, (((1,), (1,)), ((), ())), preferred_element_...  13.1 us
  transfers between devices with their start and end apart: 20, of which 16 were waited for; matrix products, arithmetic and copies ran while one was open for 17% of the time, Pallas kernels for 0%

profile of v1, /device:TPU:0, one launch (start us, length us, event | category | flops | bytes accessed | tf_op | source)
XLA Modules:
  0.0 548.4 jit_solution(10679241483964552094)
XLA Ops:
  10.0 2.3 reduce-window.6
  12.9 4.3 scatter_custom_fusion
  20.1 29.9 %all_to_all.72 = bf16[8,12,3584]{2,1,0:T(8,128)(2,1)S(1)} all-to-all(bf16[8,12,3584]{2,1,0:T(8,128)(2,1)S(1)} %get-tuple-element.37), channel_id=1, replica_groups=mesh['dp'=4,'expert'=8] {'expert'}, dimensions={0} | all-to-all | bytes 1376256 | tf_op jit(solution)/shard_map/all_to_all | solution.py:43
  53.2 16.3 %collective-permute-done = bf16[96,3584]{1,0:T(8,128)(2,1)S(1)} collective-permute-done((bf16[96,3584]{1,0:T(8,128)(2,1)S(1)}, bf16[96,3584]{1,0:T(8,128)(2,1)S(1)}, u32[]{:S(2)}, u32[]{:S(2)}) %collective-permute-start) | collective-permute-done | bytes 688160 | tf_op jit(solution)/shard_map/ppermute | solution.py:13
  70.2 14.1 %collective-permute-done.2 = bf16[96,3584]{1,0:T(8,128)(2,1)S(1)} collective-permute-done((bf16[96,3584]{1,0:T(8,128)(2,1)S(1)}, bf16[96,3584]{1,0:T(8,128)(2,1)S(1)}, u32[]{:S(2)}, u32[]{:S(2)}) %collective-permute-start.2) | collective-permute-done | bytes 688160 | tf_op jit(solution)/shard_map/ppermute | solution.py:15
  84.3 13.4 %collective-permute-done.1 = bf16[96,3584]{1,0:T(8,128)(2,1)} collective-permute-done((bf16[96,3584]{1,0:T(8,128)(2,1)S(1)}, bf16[96,3584]{1,0:T(8,128)(2,1)}, u32[]{:S(2)}, u32[]{:S(2)}) %collective-permute-start.1) | collective-permute-done | bytes 688160 | tf_op jit(solution)/shard_map/ppermute | solution.py:13
  97.7 11.4 %fusion.49 = bf16[384,3584]{1,0:T(8,128)(2,1)S(1)} fusion(s32[]{:T(128)S(6)} %select_n.56, bf16[96,3584]{1,0:T(8,128)(2,1)} %collective-permute-done.1, bf16[96,3584]{1,0:T(8,128)(2,1)S(1)} %collective-permute-done, bf16[96,3584]{1,0:T(8,128)(2,1)S(1)} %all_to_all.49, bf16[96,3584]{1,0:T(8,128)(2,1)S(1)} %collective-permute-done.2), kind=kLoop, calls=%fused_computation.95 | loop fusion | flops 22020096 | bytes 5505028 | tf_op jit(solution)/shard_map/jit(_roll_dynamic)/concatenate | solution.py:17
  112.2 2.5 multiply_convert_fusion.6
  115.4 3.1 convolution_convert_fusion.1
  118.6 26.6 %all_to_all.73 = bf16[8,12,3584]{2,1,0:T(8,128)(2,1)S(1)} all-to-all(bf16[8,12,3584]{2,1,0:T(8,128)(2,1)S(1)} %get-tuple-element.38), channel_id=1, replica_groups=mesh['dp'=4,'expert'=8] {'expert'}, dimensions={0} | all-to-all | bytes 1376256 | tf_op jit(solution)/shard_map/all_to_all | solution.py:43
  150.4 2.4 collective-permute-start.5
  152.8 19.3 %collective-permute-done.3 = bf16[96,3584]{1,0:T(8,128)(2,1)} collective-permute-done((bf16[96,3584]{1,0:T(8,128)(2,1)S(1)}, bf16[96,3584]{1,0:T(8,128)(2,1)}, u32[]{:S(2)}, u32[]{:S(2)}) %collective-permute-start.3) | collective-permute-done | bytes 688160 | tf_op jit(solution)/shard_map/ppermute | solution.py:13
  173.7 12.3 %collective-permute-done.5 = bf16[96,3584]{1,0:T(8,128)(2,1)S(1)} collective-permute-done((bf16[96,3584]{1,0:T(8,128)(2,1)S(1)}, bf16[96,3584]{1,0:T(8,128)(2,1)S(1)}, u32[]{:S(2)}, u32[]{:S(2)}) %collective-permute-start.5) | collective-permute-done | bytes 688160 | tf_op jit(solution)/shard_map/ppermute | solution.py:15
  186.1 14.1 %collective-permute-done.4 = bf16[96,3584]{1,0:T(8,128)(2,1)S(1)} collective-permute-done((bf16[96,3584]{1,0:T(8,128)(2,1)}, bf16[96,3584]{1,0:T(8,128)(2,1)S(1)}, u32[]{:S(2)}, u32[]{:S(2)}) %collective-permute-start.4) | collective-permute-done | bytes 688160 | tf_op jit(solution)/shard_map/ppermute | solution.py:13
  200.1 11.2 %fusion.42 = bf16[384,3584]{1,0:T(8,128)(2,1)S(1)} fusion(s32[]{:T(128)S(6)} %select_n.56, bf16[96,3584]{1,0:T(8,128)(2,1)S(1)} %collective-permute-done.4, bf16[96,3584]{1,0:T(8,128)(2,1)} %collective-permute-done.3, bf16[96,3584]{1,0:T(8,128)(2,1)S(1)} %all_to_all.53, bf16[96,3584]{1,0:T(8,128)(2,1)S(1)} %collective-permute-done.5), kind=kLoop, calls=%fused_computation.88 | loop fusion | flops 22020096 | bytes 5505028 | tf_op jit(solution)/shard_map/jit(_roll_dynamic)/concatenate | solution.py:17
  214.4 2.5 multiply_convert_fusion.5
  217.7 3.1 convolution_convert_fusion
  221.1 26.5 %all_to_all.74 = bf16[8,12,3584]{2,1,0:T(8,128)(2,1)S(1)} all-to-all(bf16[8,12,3584]{2,1,0:T(8,128)(2,1)S(1)} %get-tuple-element.36), channel_id=1, replica_groups=mesh['dp'=4,'expert'=8] {'expert'}, dimensions={0} | all-to-all | bytes 1376256 | tf_op jit(solution)/shard_map/all_to_all | solution.py:43
  247.9 2.9 collective-permute-start.11
  250.8 23.6 %collective-permute-done.9 = bf16[96,3584]{1,0:T(8,128)(2,1)S(1)} collective-permute-done((bf16[96,3584]{1,0:T(8,128)(2,1)S(1)}, bf16[96,3584]{1,0:T(8,128)(2,1)S(1)}, u32[]{:S(2)}, u32[]{:S(2)}) %collective-permute-start.9) | collective-permute-done | bytes 688160 | tf_op jit(solution)/shard_map/ppermute | solution.py:13
  274.8 13.6 %collective-permute-done.11 = bf16[96,3584]{1,0:T(8,128)(2,1)S(1)} collective-permute-done((bf16[96,3584]{1,0:T(8,128)(2,1)S(1)}, bf16[96,3584]{1,0:T(8,128)(2,1)S(1)}, u32[]{:S(2)}, u32[]{:S(2)}) %collective-permute-start.11) | collective-permute-done | bytes 688160 | tf_op jit(solution)/shard_map/ppermute | solution.py:15
  288.4 14.2 %collective-permute-done.10 = bf16[96,3584]{1,0:T(8,128)(2,1)S(1)} collective-permute-done((bf16[96,3584]{1,0:T(8,128)(2,1)S(1)}, bf16[96,3584]{1,0:T(8,128)(2,1)S(1)}, u32[]{:S(2)}, u32[]{:S(2)}) %collective-permute-start.10) | collective-permute-done | bytes 688160 | tf_op jit(solution)/shard_map/ppermute | solution.py:13
  302.6 11.3 %fusion.28 = bf16[384,3584]{1,0:T(8,128)(2,1)S(1)} fusion(s32[]{:T(128)S(6)} %select_n.56, bf16[96,3584]{1,0:T(8,128)(2,1)S(1)} %collective-permute-done.10, bf16[96,3584]{1,0:T(8,128)(2,1)S(1)} %collective-permute-done.9, bf16[96,3584]{1,0:T(8,128)(2,1)S(1)} %all_to_all.61, bf16[96,3584]{1,0:T(8,128)(2,1)S(1)} %collective-permute-done.11), kind=kLoop, calls=%fused_computation.74 | loop fusion | flops 22020096 | bytes 5505028 | tf_op jit(solution)/shard_map/jit(_roll_dynamic)/concatenate | solution.py:17
  319.0 3.2 fusion.1
  322.3 26.6 %all_to_all.75 = bf16[8,12,3584]{2,1,0:T(8,128)(2,1)S(1)} all-to-all(bf16[8,12,3584]{2,1,0:T(8,128)(2,1)S(1)} %get-tuple-element.35), channel_id=1, replica_groups=mesh['dp'=4,'expert'=8] {'expert'}, dimensions={0} | all-to-all | bytes 1376256 | tf_op jit(solution)/shard_map/all_to_all | solution.py:43
  349.1 2.9 collective-permute-start.8
  352.0 23.7 %collective-permute-done.6 = bf16[96,3584]{1,0:T(8,128)(2,1)S(1)} collective-permute-done((bf16[96,3584]{1,0:T(8,128)(2,1)S(1)}, bf16[96,3584]{1,0:T(8,128)(2,1)S(1)}, u32[]{:S(2)}, u32[]{:S(2)}) %collective-permute-start.6) | collective-permute-done | bytes 688160 | tf_op jit(solution)/shard_map/ppermute | solution.py:13
  375.9 13.8 %collective-permute-done.8 = bf16[96,3584]{1,0:T(8,128)(2,1)S(1)} collective-permute-done((bf16[96,3584]{1,0:T(8,128)(2,1)S(1)}, bf16[96,3584]{1,0:T(8,128)(2,1)S(1)}, u32[]{:S(2)}, u32[]{:S(2)}) %collective-permute-start.8) | collective-permute-done | bytes 688160 | tf_op jit(solution)/shard_map/ppermute | solution.py:15
  389.7 14.2 %collective-permute-done.7 = bf16[96,3584]{1,0:T(8,128)(2,1)S(1)} collective-permute-done((bf16[96,3584]{1,0:T(8,128)(2,1)S(1)}, bf16[96,3584]{1,0:T(8,128)(2,1)S(1)}, u32[]{:S(2)}, u32[]{:S(2)}) %collective-permute-start.7) | collective-permute-done | bytes 688160 | tf_op jit(solution)/shard_map/ppermute | solution.py:13
  403.8 11.3 %fusion.35 = bf16[384,3584]{1,0:T(8,128)(2,1)S(1)} fusion(s32[]{:T(128)S(6)} %select_n.56, bf16[96,3584]{1,0:T(8,128)(2,1)S(1)} %collective-permute-done.7, bf16[96,3584]{1,0:T(8,128)(2,1)S(1)} %collective-permute-done.6, bf16[96,3584]{1,0:T(8,128)(2,1)S(1)} %all_to_all.57, bf16[96,3584]{1,0:T(8,128)(2,1)S(1)} %collective-permute-done.8), kind=kLoop, calls=%fused_computation.81 | loop fusion | flops 22020096 | bytes 5505028 | tf_op jit(solution)/shard_map/jit(_roll_dynamic)/concatenate | solution.py:17
  420.5 3.1 fusion
  423.7 2.1 all_to_all.50
  425.8 3.6 all-to-all-start.1
  429.4 2.1 all_to_all.54
  431.5 21.6 %all-to-all-done.1 = bf16[8,12,3584]{2,1,0:T(8,128)(2,1)S(1)} async-done(((bf16[8,12,3584]{2,1,0:T(8,128)(2,1)}), bf16[8,12,3584]{2,1,0:T(8,128)(2,1)S(1)}, u32[]{:S(2)}, u32[]{:S(2)}) %all-to-all-start.1) | async-done | bytes 688160 | tf_op jit(solution)/shard_map/all_to_all | solution.py:49
  454.0 4.4 all-to-all-start.3
  458.4 4.1 fusion.70
  462.5 4.1 fusion.3
  468.7 13.5 %all-to-all-done.3 = bf16[8,12,3584]{2,1,0:T(8,128)(2,1)} async-done(((bf16[8,12,3584]{2,1,0:T(8,128)(2,1)}), bf16[8,12,3584]{2,1,0:T(8,128)(2,1)}, u32[]{:S(2)}, u32[]{:S(2)}) %all-to-all-start.3) | async-done | bytes 688160 | tf_op jit(solution)/shard_map/all_to_all | solution.py:49
  482.2 4.2 all-to-all-start.7
  486.5 4.0 fusion.69
  490.5 5.0 fusion.71
  495.5 4.1 fusion.2
  499.6 2.2 all_to_all.58
  501.8 8.4 %all-to-all-done.7 = bf16[8,12,3584]{2,1,0:T(8,128)(2,1)} async-done(((bf16[8,12,3584]{2,1,0:T(8,128)(2,1)}), bf16[8,12,3584]{2,1,0:T(8,128)(2,1)}, u32[]{:S(2)}, u32[]{:S(2)}) %all-to-all-start.7) | async-done | bytes 688160 | tf_op jit(solution)/shard_map/all_to_all | solution.py:49
  510.2 4.5 all-to-all-start.5
  514.8 7.1 %fusion.4 = bf16[1,512,3584]{2,1,0:T(8,128)(2,1)} fusion(f32[512,3584]{1,0:T(8,128)} %fusion.71, bf16[384,512]{1,0:T(8,128)(2,1)S(1)} %copy-done.25, bf16[384,3584]{1,0:T(8,128)(2,1)S(1)} %copy-done.16), kind=kOutput, calls=%fused_computation.48 | convolution fusion | flops 1412956160 | bytes 14155776 | tf_op jit(solution)/shard_map/dot_general | solution.py:37
  527.8 10.7 %all-to-all-done.5 = bf16[8,12,3584]{2,1,0:T(8,128)(2,1)} async-done(((bf16[8,12,3584]{2,1,0:T(8,128)(2,1)}), bf16[8,12,3584]{2,1,0:T(8,128)(2,1)}, u32[]{:S(2)}, u32[]{:S(2)}) %all-to-all-start.5) | async-done | bytes 688160 | tf_op jit(solution)/shard_map/all_to_all | solution.py:49
  (150 shorter events, 48.4 us)
Async XLA Ops:
  7.2 416.5 %reduce-scatter.5.cloned.1.call-start = ((), (), s32[]{:S(2)}) async-start(), calls=%async_computation.12 | async-start | bytes 3440640 | tf_op jit(solution)/shard_map/reduce_scatter | solution.py:48
  50.2 19.3 %collective-permute-start = (bf16[96,3584]{1,0:T(8,128)(2,1)S(1)}, bf16[96,3584]{1,0:T(8,128)(2,1)S(1)}, u32[]{:S(2)}, u32[]{:S(2)}) collective-permute-start(bf16[96,3584]{1,0:T(8,128)(2,1)S(1)} %all_to_all.49), channel_id=1, source_target_pairs={{0,8},{8,16},{16,24},{24,0},{1,9},{9,17},{17,25},{25,1},{2,10},{10... | collective-permute-start | bytes 2064392 | tf_op jit(solution)/shard_map/ppermute | solution.py:13
  51.7 32.6 %collective-permute-start.2 = (bf16[96,3584]{1,0:T(8,128)(2,1)S(1)}, bf16[96,3584]{1,0:T(8,128)(2,1)S(1)}, u32[]{:S(2)}, u32[]{:S(2)}) collective-permute-start(bf16[96,3584]{1,0:T(8,128)(2,1)S(1)} %all_to_all.49), channel_id=1, source_target_pairs={{0,24},{8,0},{16,8},{24,16},{1,25},{9,1},{17,9},{25,17},{2,26},{10... | collective-permute-start | bytes 2064392 | tf_op jit(solution)/shard_map/ppermute | solution.py:15
  69.5 28.2 %collective-permute-start.1 = (bf16[96,3584]{1,0:T(8,128)(2,1)S(1)}, bf16[96,3584]{1,0:T(8,128)(2,1)}, u32[]{:S(2)}, u32[]{:S(2)}) collective-permute-start(bf16[96,3584]{1,0:T(8,128)(2,1)S(1)} %collective-permute-done), channel_id=1, source_target_pairs={{0,8},{8,16},{16,24},{24,0},{1,9},{9,17},{17,25},{25,1},{2,10},{10... | collective-permute-start | bytes 2064392 | tf_op jit(solution)/shard_map/ppermute | solution.py:13
  70.2 38.9 %copy-start.3 = (bf16[1,3584,512]{2,1,0:T(8,128)(2,1)S(1)}, bf16[1,3584,512]{2,1,0:T(8,128)(2,1)}, u32[]{:S(2)}) copy-start(bf16[1,3584,512]{2,1,0:T(8,128)(2,1)} %param.13) | copy-start | bytes 11010052
  109.1 3.0 copy-start.7
  112.2 2.5 copy-start.33
  112.2 3.2 copy-start.29
  118.6 27.4 %copy-start.28 = (f32[128,8]{0,1:T(8,128)S(1)}, f32[128,8]{0,1:T(8,128)}, u32[]{:S(2)}) copy-start(f32[128,8]{0,1:T(8,128)} %param.10) | copy-start | bytes 12292
  118.6 310.8 %reduce-scatter.7.cloned.1.call-start = ((), (), s32[]{:S(2)}) async-start(), calls=%async_computation.13 | async-start | bytes 3440640 | tf_op jit(solution)/shard_map/reduce_scatter | solution.py:48
  145.3 26.8 %collective-permute-start.3 = (bf16[96,3584]{1,0:T(8,128)(2,1)S(1)}, bf16[96,3584]{1,0:T(8,128)(2,1)}, u32[]{:S(2)}, u32[]{:S(2)}) collective-permute-start(bf16[96,3584]{1,0:T(8,128)(2,1)S(1)} %all_to_all.53), channel_id=1, source_target_pairs={{0,8},{8,16},{16,24},{24,0},{1,9},{9,17},{17,25},{25,1},{2,10},{10... | collective-permute-start | bytes 2064392 | tf_op jit(solution)/shard_map/ppermute | solution.py:13
  150.4 60.9 %copy-start.11 = (bf16[192,3584]{1,0:T(8,128)(2,1)}, bf16[192,3584]{1,0:T(8,128)(2,1)S(1)}, u32[]{:S(2)}) copy-start(bf16[192,3584]{1,0:T(8,128)(2,1)S(1)} %gather_fusion.2) | copy-start | bytes 4128772
  150.4 35.7 %collective-permute-start.5 = (bf16[96,3584]{1,0:T(8,128)(2,1)S(1)}, bf16[96,3584]{1,0:T(8,128)(2,1)S(1)}, u32[]{:S(2)}, u32[]{:S(2)}) collective-permute-start(bf16[96,3584]{1,0:T(8,128)(2,1)S(1)} %all_to_all.53), channel_id=1, source_target_pairs={{0,24},{8,0},{16,8},{24,16},{1,25},{9,1},{17,9},{25,17},{2,26},{10... | collective-permute-start | bytes 2064392 | tf_op jit(solution)/shard_map/ppermute | solution.py:15
  172.1 28.0 %collective-permute-start.4 = (bf16[96,3584]{1,0:T(8,128)(2,1)}, bf16[96,3584]{1,0:T(8,128)(2,1)S(1)}, u32[]{:S(2)}, u32[]{:S(2)}) collective-permute-start(bf16[96,3584]{1,0:T(8,128)(2,1)} %collective-permute-done.3), channel_id=1, source_target_pairs={{0,8},{8,16},{16,24},{24,0},{1,9},{9,17},{17,25},{25,1},{2,10},{10... | collective-permute-start | bytes 2064392 | tf_op jit(solution)/shard_map/ppermute | solution.py:13
  172.3 39.0 %copy-start.4 = (bf16[1,3584,512]{2,1,0:T(8,128)(2,1)S(1)}, bf16[1,3584,512]{2,1,0:T(8,128)(2,1)}, u32[]{:S(2)}) copy-start(bf16[1,3584,512]{2,1,0:T(8,128)(2,1)} %param.13) | copy-start | bytes 11010052
  211.4 3.0 copy-start.8
  214.4 3.2 copy-start.30
  217.6 3.2 copy-start.17
  220.8 245.8 %reduce-scatter.11.cloned.1.call-start = ((), (), s32[]{:S(2)}) async-start(), calls=%async_computation.15 | async-start | bytes 3440640 | tf_op jit(solution)/shard_map/reduce_scatter | solution.py:48
  247.8 66.1 %copy-start.31 = (bf16[1,512,3584]{2,1,0:T(8,128)(2,1)S(1)}, bf16[1,512,3584]{2,1,0:T(8,128)(2,1)}, u32[]{:S(2)}) copy-start(bf16[1,512,3584]{2,1,0:T(8,128)(2,1)} %param.15) | copy-start | bytes 11010052
  247.8 66.1 %copy-start.36 = (f32[384,512]{1,0:T(8,128)S(1)}, f32[384,512]{1,0:T(8,128)}, u32[]{:S(2)}) copy-start(f32[384,512]{1,0:T(8,128)} %copy-done.35) | copy-start | bytes 2359300
  247.8 66.1 %copy-start.38 = (f32[384,512]{1,0:T(8,128)S(1)}, f32[384,512]{1,0:T(8,128)}, u32[]{:S(2)}) copy-start(f32[384,512]{1,0:T(8,128)} %get-tuple-element.19) | copy-start | bytes 2359300
  247.8 26.5 %collective-permute-start.9 = (bf16[96,3584]{1,0:T(8,128)(2,1)S(1)}, bf16[96,3584]{1,0:T(8,128)(2,1)S(1)}, u32[]{:S(2)}, u32[]{:S(2)}) collective-permute-start(bf16[96,3584]{1,0:T(8,128)(2,1)S(1)} %all_to_all.61), channel_id=1, source_target_pairs={{0,8},{8,16},{16,24},{24,0},{1,9},{9,17},{17,25},{25,1},{2,10},{10... | collective-permute-start | bytes 2064392 | tf_op jit(solution)/shard_map/ppermute | solution.py:13
  247.9 40.5 %collective-permute-start.11 = (bf16[96,3584]{1,0:T(8,128)(2,1)S(1)}, bf16[96,3584]{1,0:T(8,128)(2,1)S(1)}, u32[]{:S(2)}, u32[]{:S(2)}) collective-permute-start(bf16[96,3584]{1,0:T(8,128)(2,1)S(1)} %all_to_all.61), channel_id=1, source_target_pairs={{0,24},{8,0},{16,8},{24,16},{1,25},{9,1},{17,9},{25,17},{2,26},{10... | collective-permute-start | bytes 2064392 | tf_op jit(solution)/shard_map/ppermute | solution.py:15
  274.4 28.3 %collective-permute-start.10 = (bf16[96,3584]{1,0:T(8,128)(2,1)S(1)}, bf16[96,3584]{1,0:T(8,128)(2,1)S(1)}, u32[]{:S(2)}, u32[]{:S(2)}) collective-permute-start(bf16[96,3584]{1,0:T(8,128)(2,1)S(1)} %collective-permute-done.9), channel_id=1, source_target_pairs={{0,8},{8,16},{16,24},{24,0},{1,9},{9,17},{17,25},{25,1},{2,10},{10... | collective-permute-start | bytes 2064392 | tf_op jit(solution)/shard_map/ppermute | solution.py:13
  314.0 3.0 copy-start.5
  322.2 177.4 %reduce-scatter.9.cloned.1.call-start = ((), (), s32[]{:S(2)}) async-start(), calls=%async_computation.14 | async-start | bytes 3440640 | tf_op jit(solution)/shard_map/reduce_scatter | solution.py:48
  349.0 66.1 %copy-start.32 = (bf16[1,512,3584]{2,1,0:T(8,128)(2,1)S(1)}, bf16[1,512,3584]{2,1,0:T(8,128)(2,1)}, u32[]{:S(2)}) copy-start(bf16[1,512,3584]{2,1,0:T(8,128)(2,1)} %param.15) | copy-start | bytes 11010052
  349.0 66.1 %copy-start.34 = (f32[384,512]{1,0:T(8,128)S(1)}, f32[384,512]{1,0:T(8,128)}, u32[]{:S(2)}) copy-start(f32[384,512]{1,0:T(8,128)} %copy-done.33) | copy-start | bytes 2359300
  349.0 66.1 %copy-start.37 = (f32[384,512]{1,0:T(8,128)S(1)}, f32[384,512]{1,0:T(8,128)}, u32[]{:S(2)}) copy-start(f32[384,512]{1,0:T(8,128)} %get-tuple-element.17) | copy-start | bytes 2359300
  349.0 26.7 %collective-permute-start.6 = (bf16[96,3584]{1,0:T(8,128)(2,1)S(1)}, bf16[96,3584]{1,0:T(8,128)(2,1)S(1)}, u32[]{:S(2)}, u32[]{:S(2)}) collective-permute-start(bf16[96,3584]{1,0:T(8,128)(2,1)S(1)} %all_to_all.57), channel_id=1, source_target_pairs={{0,8},{8,16},{16,24},{24,0},{1,9},{9,17},{17,25},{25,1},{2,10},{10... | collective-permute-start | bytes 2064392 | tf_op jit(solution)/shard_map/ppermute | solution.py:13
  349.1 40.6 %collective-permute-start.8 = (bf16[96,3584]{1,0:T(8,128)(2,1)S(1)}, bf16[96,3584]{1,0:T(8,128)(2,1)S(1)}, u32[]{:S(2)}, u32[]{:S(2)}) collective-permute-start(bf16[96,3584]{1,0:T(8,128)(2,1)S(1)} %all_to_all.57), channel_id=1, source_target_pairs={{0,24},{8,0},{16,8},{24,16},{1,25},{9,1},{17,9},{25,17},{2,26},{10... | collective-permute-start | bytes 2064392 | tf_op jit(solution)/shard_map/ppermute | solution.py:15
  375.7 28.1 %collective-permute-start.7 = (bf16[96,3584]{1,0:T(8,128)(2,1)S(1)}, bf16[96,3584]{1,0:T(8,128)(2,1)S(1)}, u32[]{:S(2)}, u32[]{:S(2)}) collective-permute-start(bf16[96,3584]{1,0:T(8,128)(2,1)S(1)} %collective-permute-done.6), channel_id=1, source_target_pairs={{0,8},{8,16},{16,24},{24,0},{1,9},{9,17},{17,25},{25,1},{2,10},{10... | collective-permute-start | bytes 2064392 | tf_op jit(solution)/shard_map/ppermute | solution.py:13
  415.1 3.3 copy-start.6
  417.0 3.1 copy-start.20
  417.0 3.1 copy-start.22
  425.8 27.3 %all-to-all-start.1 = ((bf16[8,12,3584]{2,1,0:T(8,128)(2,1)}), bf16[8,12,3584]{2,1,0:T(8,128)(2,1)S(1)}, u32[]{:S(2)}, u32[]{:S(2)}) async-start(bf16[8,12,3584]{2,1,0:T(8,128)(2,1)} %all_to_all.50), calls=%async_computation.2 | async-start | bytes 1835008 | tf_op jit(solution)/shard_map/all_to_all | solution.py:49
  454.0 28.2 %all-to-all-start.3 = ((bf16[8,12,3584]{2,1,0:T(8,128)(2,1)}), bf16[8,12,3584]{2,1,0:T(8,128)(2,1)}, u32[]{:S(2)}, u32[]{:S(2)}) async-start(bf16[8,12,3584]{2,1,0:T(8,128)(2,1)} %all_to_all.54), calls=%async_computation.5 | async-start | bytes 1835008 | tf_op jit(solution)/shard_map/all_to_all | solution.py:49
  458.4 4.1 copy-start.1
  458.4 4.1 copy-start.23
  482.2 28.0 %all-to-all-start.7 = ((bf16[8,12,3584]{2,1,0:T(8,128)(2,1)}), bf16[8,12,3584]{2,1,0:T(8,128)(2,1)}, u32[]{:S(2)}, u32[]{:S(2)}) async-start(bf16[8,12,3584]{2,1,0:T(8,128)(2,1)} %all_to_all.62), calls=%async_computation.11 | async-start | bytes 1835008 | tf_op jit(solution)/shard_map/all_to_all | solution.py:49
  486.5 4.1 copy-start.14
  486.5 4.1 copy-start.27
  490.5 5.0 copy-start.21
  499.6 15.1 %copy-start.16 = (bf16[384,3584]{1,0:T(8,128)(2,1)S(1)}, bf16[384,3584]{1,0:T(8,128)(2,1)}, u32[]{:S(2)}) copy-start(bf16[384,3584]{1,0:T(8,128)(2,1)} %copy-done.15) | copy-start | bytes 8257540
  499.6 15.2 %copy-start.25 = (bf16[384,512]{1,0:T(8,128)(2,1)S(1)}, bf16[384,512]{1,0:T(8,128)(2,1)}, u32[]{:S(2)}) copy-start(bf16[384,512]{1,0:T(8,128)(2,1)} %copy-done.24) | copy-start | bytes 1179652
  510.2 28.3 %all-to-all-start.5 = ((bf16[8,12,3584]{2,1,0:T(8,128)(2,1)}), bf16[8,12,3584]{2,1,0:T(8,128)(2,1)}, u32[]{:S(2)}, u32[]{:S(2)}) async-start(bf16[8,12,3584]{2,1,0:T(8,128)(2,1)} %all_to_all.58), calls=%async_computation.8 | async-start | bytes 1835008 | tf_op jit(solution)/shard_map/all_to_all | solution.py:49
  514.8 7.1 %copy-start.19 = (bf16[8,12,3584]{2,1,0:T(8,128)(2,1)S(1)}, bf16[8,12,3584]{2,1,0:T(8,128)(2,1)}, u32[]{:S(2)}) copy-start(bf16[8,12,3584]{2,1,0:T(8,128)(2,1)} %copy-done.18) | copy-start | bytes 2064388
  (11 other events, 17.6 us)
Sparse Core Ops, SparseCore 0:
  118.7 47.3 reduce-scatter.4
  220.9 47.3 reduce-scatter.6
  322.3 47.2 reduce-scatter.10
  423.8 39.0 reduce-scatter.8
